TPU v7x, 32 devices: a whole 2x2x4 slice. The times are simulated.
32 devices in a mesh: fsdp: 4 (over y, x), seq: 8 (over z, core).
Axes of the slice: x: 2, y: 2, z: 4, core: 2. Of those that a mesh axis runs over, the one named last changes fastest.
Arguments:
- events: bfloat16 [4, 1024, 2048], P('fsdp', 'seq'), may hold values from -6 to 6
- type_ids: int32 [4, 1024], P('fsdp', 'seq'), may hold values from 0 to 255
- type_table: bfloat16 [256, 2048], P('fsdp'), may hold values from -6 to 6
- norm_gain: float32 [2048], replicated, may hold values from 0.25 to 1.75
- kernel: bfloat16 [2048, 1152], P('fsdp'), may hold values from -0.1875 to 0.1875
- upstream: bfloat16 [4, 1024, 2048], P('fsdp', 'seq'), may hold values from -6 to 6
Outputs:
- input_grad: bfloat16 [4, 1024, 2048], P('fsdp', 'seq')
- table_grad: float32 [256, 2048], P(('fsdp', 'seq'))
- gain_grad: float32 [2048], P(('fsdp', 'seq'))
- kernel_grad: float32 [2048, 1152], P('seq')
All inputs are finite; a program needn't handle non-finite values.
Results may differ from a plain program's by a relative error of at most 0.0053.
Values may be sent and summed in bfloat16 or wider, within the bound.
No kernel may reach another device: no remote copies, remote signals or barrier semaphores. Data moves between devices by JAX's collectives and lax.ppermute only.
A program may use at most 128 MiB of HBM per device.

v0:
```python
import jax
import jax.numpy as jnp
from jax import lax
from jax.sharding import PartitionSpec as P

GROUPS = 16
KERNEL = 9


def with_halo(cells, sides, width):
    for axis, dim in sides:
        count = lax.axis_size(axis)
        ends = count - 1
        head = lax.slice_in_dim(cells, 0, width, axis=dim)
        tail = lax.slice_in_dim(cells, cells.shape[dim] - width, cells.shape[dim], axis=dim)
        cells = jnp.concatenate(
            [
                lax.ppermute(tail, axis, [(i, (i + 1) % count) for i in range(ends)]),
                cells,
                lax.ppermute(head, axis, [((i + 1) % count, i) for i in range(ends)]),
            ],
            axis=dim,
        )
    return cells


def from_partner(value, axis, apart):
    mask = 2**apart
    pairs = [(source, source ^ mask) for source in range(lax.axis_size(axis))]
    return lax.ppermute(value, axis, pairs)


def gather_rows(block, axis):
    count = lax.axis_size(axis)
    return lax.all_to_all(jnp.tile(block, (count, 1)), axis, 0, 0, tiled=True)


def sum_rows(block, axis):
    count = lax.axis_size(axis)
    parts = block.reshape(count, block.shape[0] // count, *block.shape[1:])
    return lax.all_to_all(parts, axis, 0, 0, tiled=True).sum(axis=0)


def psum_rows(block, axis):
    return gather_rows(sum_rows(block, axis), axis)


def scatter_terms(table_term, gain_term):
    fsdp = lax.axis_size("fsdp")
    seq = lax.axis_size("seq")
    types, width = table_term.shape
    wide = width // fsdp
    gain_rows = (
        jnp.zeros((fsdp, 1, width), jnp.float32).at[:, 0, :wide].set(gain_term.reshape(fsdp, wide))
    )
    first = jnp.concatenate([table_term.reshape(fsdp, types // fsdp, width), gain_rows], axis=1)
    first = lax.all_to_all(first, "fsdp", 0, 0, tiled=True).sum(axis=0)
    rows = types // fsdp
    narrow = wide // seq
    gain_rows = (
        jnp.zeros((seq, 1, width), jnp.float32)
        .at[:, 0, :narrow]
        .set(first[rows, :wide].reshape(seq, narrow))
    )
    second = jnp.concatenate([first[:rows].reshape(seq, rows // seq, width), gain_rows], axis=1)
    second = lax.all_to_all(second, "seq", 0, 0, tiled=True).sum(axis=0)
    return (second[: rows // seq], second[rows // seq, :narrow])


def body(events, type_ids, type_table, norm_gain, kernel, upstream):
    length = events.shape[1]
    width = events.shape[2]
    chans = width // GROUPS
    half = KERNEL // 2
    seq_count = lax.axis_size("seq")
    total = length * seq_count * lax.axis_size("fsdp")
    scale = 1.0 / jnp.sqrt(jnp.float32(total))
    table = gather_rows(type_table, "fsdp")
    onehot = (type_ids[0][:, None] == jnp.arange(table.shape[0], dtype=jnp.int32)[None, :]).astype(
        jnp.bfloat16
    )
    mixed = events[0].astype(jnp.float32) + jnp.dot(
        onehot, table, preferred_element_type=jnp.float32
    )
    inv = lax.rsqrt(jnp.mean(mixed * mixed, axis=-1, keepdims=True) + 1e-06)
    normed = (mixed * inv * norm_gain).astype(jnp.bfloat16)
    padded = with_halo(normed, (("seq", 0),), half)
    padded = padded.reshape(length + 2 * half, GROUPS, chans)
    weights = lax.all_gather(kernel, "fsdp", axis=0, tiled=True).reshape(
        GROUPS, chans, KERNEL, chans
    )
    conv = jnp.zeros((length, GROUPS, chans), jnp.float32)
    for k in range(KERNEL):
        conv = conv + jnp.einsum(
            "tgc,goc->tgo",
            padded[k : k + length],
            weights[:, :, k, :],
            preferred_element_type=jnp.float32,
        )
    up_float = upstream[0].astype(jnp.float32)
    sig = jax.nn.sigmoid(conv)
    dconv = (up_float.reshape(length, GROUPS, chans) * sig * (1.0 + conv * (1.0 - sig))).astype(
        jnp.bfloat16
    )
    dflat = dconv.reshape(length, width)
    dpad = with_halo(dflat, (("seq", 0),), half)
    dpad = dpad.reshape(length + 2 * half, GROUPS, chans)
    dnormed = jnp.zeros((length, GROUPS, chans), jnp.float32)
    for k in range(KERNEL):
        dnormed = dnormed + jnp.einsum(
            "tgo,goc->tgc",
            dpad[2 * half - k : 2 * half - k + length],
            weights[:, :, k, :],
            preferred_element_type=jnp.float32,
        )
    slice_width = width // seq_count
    normed_slice, dconv_slice = (
        lax.all_to_all(normed, "seq", split_axis=1, concat_axis=0, tiled=True),
        lax.all_to_all(dflat, "seq", split_axis=1, concat_axis=0, tiled=True),
    )
    whole = normed_slice.shape[0]
    if slice_width < chans:
        spread = chans // slice_width
        position = lax.axis_index("seq")
        group_rows = normed_slice
        for bit in range(spread.bit_length() - 1):
            partner = from_partner(group_rows, "seq", bit)
            lower = position >> bit & 1 == 0
            group_rows = jnp.where(
                lower,
                jnp.concatenate([group_rows, partner], axis=1),
                jnp.concatenate([partner, group_rows], axis=1),
            )
        group_in = group_rows.reshape(whole, 1, chans)
        group_out = dconv_slice.reshape(whole, 1, slice_width)
    else:
        local_groups = slice_width // chans
        group_in = normed_slice.reshape(whole, local_groups, chans)
        group_out = dconv_slice.reshape(whole, local_groups, chans)
    group_pad = jnp.pad(group_in, ((half, half), (0, 0), (0, 0)))
    kterms = []
    for k in range(KERNEL):
        kterms.append(
            jnp.einsum(
                "tgo,tgc->goc",
                group_out,
                group_pad[k : k + whole],
                preferred_element_type=jnp.float32,
            )
        )
    kernel_part = jnp.stack(kterms, axis=2).reshape(slice_width, KERNEL * chans) * scale
    kernel_grad = psum_rows(kernel_part, "fsdp")
    dnormed = dnormed.reshape(length, width)
    gain_term = jnp.sum(dnormed * mixed * inv, axis=0) * scale
    scaled = norm_gain * dnormed
    dmixed = inv * scaled - mixed * inv * inv * inv * jnp.mean(
        scaled * mixed, axis=-1, keepdims=True
    )
    input_grad = (up_float + dmixed).astype(jnp.bfloat16)
    table_term = (
        lax.dot_general(
            onehot, input_grad, (((0,), (0,)), ((), ())), preferred_element_type=jnp.float32
        )
        * scale
    )
    table_grad, gain_grad = scatter_terms(table_term, gain_term)
    return (input_grad[None], table_grad, gain_grad, kernel_grad)


def solution(mesh):
    return jax.shard_map(
        body,
        mesh=mesh,
        in_specs=(
            P("fsdp", "seq", None),
            P("fsdp", "seq"),
            P("fsdp", None),
            P(),
            P("fsdp", None),
            P("fsdp", "seq", None),
        ),
        out_specs=(
            P("fsdp", "seq", None),
            P(("fsdp", "seq"), None),
            P(("fsdp", "seq")),
            P("seq", None),
        ),
        check_vma=False,
    )
```

profile of v0, /device:TPU:0, one launch (start us, length us, event | category | flops | bytes accessed | tf_op | source)
XLA Modules:
  0.0 257.1 jit_solution(17122217566961818963)
XLA Ops:
  8.3 23.8 %all_to_all.65 = bf16[4,64,2048]{2,1,0:T(8,128)(2,1)S(1)} all-to-all(bf16[4,64,2048]{2,1,0:T(8,128)(2,1)S(1)} %tile.4), channel_id=1, replica_groups=mesh['fsdp'=4,'seq'=8] {'fsdp'}, dimensions={0} | all-to-all | bytes 2097152 | tf_op jit(solution)/shard_map/all_to_all | solution.py:35
  33.9 5.2 %all-to-all-start.4 = ((bf16[128,8,256]{0,2,1:T(8,128)(2,1)}), bf16[128,8,256]{0,2,1:T(8,128)(2,1)S(1)}, u32[]{:S(2)}, u32[]{:S(2)}) async-start(bf16[128,8,256]{0,2,1:T(8,128)(2,1)} %bitcast.35), calls=%async_computation.4 | async-start | bytes 1048576 | tf_op jit(solution)/shard_map/all_to_all | solution.py:118
  39.1 2.4 collective-permute-start
  44.0 1.6 collective-permute-done.1
  45.7 2.7 %fusion.52 = (bf16[16,16,8,128]{3,2,1,0:T(8,128)(2,1)}, bf16[16,16,8,128]{3,2,1,0:T(8,128)(2,1)}, bf16[16,16,8,128]{3,2,1,0:T(8,128)(2,1)}, bf16[16,16,8,128]{3,...) fusion(bf16[4,2048]{1,0:T(4,128)(2,1)S(1)} %collective-permute-, ...), kind=kLoop, calls=%fused_computation.112 | loop fusion | flops 8388608 | bytes 4751360
  48.3 6.1 %all-to-all-done.4 = bf16[128,8,256]{0,2,1:T(8,128)(2,1)S(1)} async-done(((bf16[128,8,256]{0,2,1:T(8,128)(2,1)}), bf16[128,8,256]{0,2,1:T(8,128)(2,1)S(1)}, u32[]{:S(2)}, u32[]{:S(2)}) %all-to-all-start.4) | async-done | bytes 524320 | tf_op jit(solution)/shard_map/all_to_all | solution.py:118
  56.0 17.2 %all-gather.2.cloned.1.call-done = bf16[2048,1152]{1,0:T(8,128)(2,1)} async-done(((bf16[512,1152]{1,0:T(8,128)(2,1)}), bf16[2048,1152]{1,0:T(8,128)(2,1)}) %all-gather.2.cloned.1.call-update) | async-done | bytes 4718608 | tf_op jit(solution)/shard_map/all_gather | solution.py:89
  73.1 10.5 %reshape.199 = bf16[16,128,9,128]{3,2,1,0:T(8,128)(2,1)} reshape(bf16[2048,1152]{1,0:T(8,128)(2,1)} %all-gather.2.cloned.1.call-done) | data formatting | bytes 9437184 | tf_op jit(solution)/shard_map/reshape | solution.py:89
  83.6 19.7 %fusion.82 = (bf16[16,128,1,128]{3,2,1,0:T(2,128)(2,1)S(1)}, bf16[16,128,1,128]{3,2,1,0:T(2,128)(2,1)S(1)}, bf16[16,128,1,128]{3,2,1,0:T(2,128)(2,1)S(1)}, bf16[...) fusion(bf16[16,128,9,128]{3,2,1,0:T(8,128)(2,1)} %reshape.199), kind=kLoop, calls=%fused_computation.160 | loop fusion | bytes 9437184 | tf_op jit(solution)/shard_map/slice | solution.py:97
  115.5 3.9 %collective-permute-start.3 = (bf16[4,2048]{0,1:T(8,128)(2,1)}, bf16[4,2048]{0,1:T(8,128)(2,1)}, u32[]{:S(2)}, u32[]{:S(2)}) collective-permute-start(bf16[4,2048]{0,1:T(8,128)(2,1)} %copy.253), channel_id=1, source_target_pairs={{0,1},{1,2},{2,3},{3,4},{4,5},{5,6},{6,7},{8,9},{9,10},{10,11},{11... | collective-permute-start | bytes 49160 | tf_op jit(solution)/shard_map/ppermute | solution.py:18
  119.3 2.7 %fusion.63 = f32[16,128,128]{1,2,0:T(8,128)} fusion(bf16[128,16,128]{2,0,1:T(8,128)(2,1)S(1)} %fusion.14, bf16[16,128,1,128]{3,2,1,0:T(2,128)(2,1)} %copy-done.12), kind=kOutput, calls=%fused_computation.133 | convolution fusion | flops 67108864 | bytes 2097152 | tf_op jit(solution)/shard_map/tgo,goc->tgc/dot_general | solution.py:110
  123.1 4.6 %all-to-all-start.3 = ((bf16[128,8,256]{0,2,1:T(8,128)(2,1)}), bf16[128,8,256]{0,2,1:T(8,128)(2,1)}, u32[]{:S(2)}, u32[]{:S(2)}) async-start(bf16[128,8,256]{0,2,1:T(8,128)(2,1)} %bitcast.33), calls=%async_computation.3 | async-start | bytes 1048576 | tf_op jit(solution)/shard_map/all_to_all | solution.py:119
  127.7 6.5 %pad_maximum_fusion = (bf16[128,2048]{0,1:T(8,128)(2,1)S(1)}, bf16[128,2048]{0,1:T(8,128)(2,1)S(1)}, bf16[128,2048]{0,1:T(8,128)(2,1)S(1)}, bf16[128,2048]{0,1:T...) fusion(bf16[128,2048]{0,1:T(8,128)(2,1)} %bitcast.14, ...), kind=kLoop, calls=%fused_computation.109 | loop fusion | flops 8388608 | bytes 4751360 | tf_op jit(solution)/shard_map/concatenate | solution.py:16
  145.2 1.7 select_maximum_fusion
  146.8 3.6 %all-to-all-start.1 = ((f32[4,65,2048]{2,1,0:T(8,128)}), f32[4,65,2048]{2,1,0:T(8,128)S(1)}, u32[]{:S(2)}, u32[]{:S(2)}) async-start(f32[4,65,2048]{2,1,0:T(8,128)} %select_maximum_fusion), calls=%async_computation.1 | async-start | bytes 4718592 | tf_op jit(solution)/shard_map/all_to_all | solution.py:57
  156.6 2.1 copy.270
  158.7 2.5 mul.133
  161.2 17.9 %all-to-all-done.1 = f32[4,65,2048]{2,1,0:T(8,128)S(1)} async-done(((f32[4,65,2048]{2,1,0:T(8,128)}), f32[4,65,2048]{2,1,0:T(8,128)S(1)}, u32[]{:S(2)}, u32[]{:S(2)}) %all-to-all-start.1) | async-done | bytes 2129952 | tf_op jit(solution)/shard_map/all_to_all | solution.py:57
  179.1 4.3 %all-to-all-start.5 = ((f32[4,64,1152]{2,1,0:T(8,128)}), f32[4,64,1152]{2,1,0:T(8,128)}, u32[]{:S(2)}, u32[]{:S(2)}) async-start(f32[4,64,1152]{2,1,0:T(8,128)} %mul.133), calls=%async_computation.5 | async-start | bytes 2359296 | tf_op jit(solution)/shard_map/all_to_all | solution.py:41
  184.8 13.9 %all-to-all-done.5 = f32[4,64,1152]{2,1,0:T(8,128)} async-done(((f32[4,64,1152]{2,1,0:T(8,128)}), f32[4,64,1152]{2,1,0:T(8,128)}, u32[]{:S(2)}, u32[]{:S(2)}) %all-to-all-start.5) | async-done | bytes 1179680 | tf_op jit(solution)/shard_map/all_to_all | solution.py:41
  198.6 4.3 %all-to-all-start.2 = ((f32[8,9,2048]{2,1,0:T(8,128)}), f32[8,9,2048]{2,1,0:T(8,128)S(1)}, u32[]{:S(2)}, u32[]{:S(2)}) async-start(f32[8,9,2048]{2,1,0:T(8,128)} %select_maximum_fusion.1), calls=%async_computation.2 | async-start | bytes 2097152 | tf_op jit(solution)/shard_map/all_to_all | solution.py:66
  204.3 25.2 %all-to-all-done.2 = f32[8,9,2048]{2,1,0:T(8,128)S(1)} async-done(((f32[8,9,2048]{2,1,0:T(8,128)}), f32[8,9,2048]{2,1,0:T(8,128)S(1)}, u32[]{:S(2)}, u32[]{:S(2)}) %all-to-all-start.2) | async-done | bytes 589856 | tf_op jit(solution)/shard_map/all_to_all | solution.py:66
  230.6 3.5 %all-to-all-start.6 = ((f32[4,64,1152]{2,1,0:T(8,128)}), f32[4,64,1152]{2,1,0:T(8,128)S(1)}, u32[]{:S(2)}, u32[]{:S(2)}) async-start(f32[4,64,1152]{2,1,0:T(8,128)} %tile.5), calls=%async_computation.6 | async-start | bytes 2359296 | tf_op jit(solution)/shard_map/all_to_all | solution.py:35
  235.4 13.9 %all-to-all-done.6 = f32[4,64,1152]{2,1,0:T(8,128)S(1)} async-done(((f32[4,64,1152]{2,1,0:T(8,128)}), f32[4,64,1152]{2,1,0:T(8,128)S(1)}, u32[]{:S(2)}, u32[]{:S(2)}) %all-to-all-start.6) | async-done | bytes 1179680 | tf_op jit(solution)/shard_map/all_to_all | solution.py:35
  (137 shorter events, 42.8 us)
Async XLA Ops:
  7.2 66.0 %all-gather.2.cloned.1.call-start = ((), (), s32[]{:S(2)}) async-start(), calls=%async_computation.7 | async-start | bytes 5898240 | tf_op jit(solution)/shard_map/all_gather | solution.py:89
  8.2 23.8 %copy-start.28 = (bf16[1,128,2048]{2,1,0:T(8,128)(2,1)S(1)}, bf16[1,128,2048]{2,1,0:T(8,128)(2,1)}, u32[]{:S(2)}) copy-start(bf16[1,128,2048]{2,1,0:T(8,128)(2,1)} %param.10) | copy-start | bytes 1572868
  8.2 23.8 %copy-start.33 = (s32[1,128]{1,0:T(1,128)S(1)}, s32[1,128]{1,0:T(1,128)}, u32[]{:S(2)}) copy-start(s32[1,128]{1,0:T(1,128)} %param.11) | copy-start | bytes 1540
  32.9 9.9 %copy-start.18 = (bf16[1,128,2048]{2,1,0:T(8,128)(2,1)S(1)}, bf16[1,128,2048]{2,1,0:T(8,128)(2,1)}, u32[]{:S(2)}) copy-start(bf16[1,128,2048]{2,1,0:T(8,128)(2,1)} %param.15) | copy-start | bytes 1572868
  33.9 20.5 %all-to-all-start.4 = ((bf16[128,8,256]{0,2,1:T(8,128)(2,1)}), bf16[128,8,256]{0,2,1:T(8,128)(2,1)S(1)}, u32[]{:S(2)}, u32[]{:S(2)}) async-start(bf16[128,8,256]{0,2,1:T(8,128)(2,1)} %bitcast.35), calls=%async_computation.4 | async-start | bytes 1048576 | tf_op jit(solution)/shard_map/all_to_all | solution.py:118
  39.1 5.0 %collective-permute-start = (bf16[4,2048]{1,0:T(4,128)(2,1)S(1)}, bf16[4,2048]{1,0:T(4,128)(2,1)S(1)}, u32[]{:S(2)}, u32[]{:S(2)}) collective-permute-start(bf16[4,2048]{1,0:T(4,128)(2,1)S(1)} %get-tuple-element.66), channel_id=1, source_target_pairs={{0,1},{1,2},{2,3},{3,4},{4,5},{5,6},{6,7},{8,9},{9,10},{10,11},{11... | collective-permute-start | bytes 49160 | tf_op jit(solution)/shard_map/ppermute | solution.py:18
  41.5 4.2 %collective-permute-start.1 = (bf16[4,2048]{1,0:T(4,128)(2,1)S(1)}, bf16[4,2048]{1,0:T(4,128)(2,1)S(1)}, u32[]{:S(2)}, u32[]{:S(2)}) collective-permute-start(bf16[4,2048]{1,0:T(4,128)(2,1)S(1)} %get-tuple-element.65), channel_id=1, source_target_pairs={{1,0},{2,1},{3,2},{4,3},{5,4},{6,5},{7,6},{9,8},{10,9},{11,10},{12... | collective-permute-start | bytes 49160 | tf_op jit(solution)/shard_map/ppermute | solution.py:20
  55.0 28.6 %copy-start = (bf16[1024,2,128]{0,2,1:T(8,128)(2,1)}, bf16[1024,2,128]{0,2,1:T(8,128)(2,1)S(1)}, u32[]{:S(2)}) copy-start(bf16[1024,2,128]{0,2,1:T(8,128)(2,1)S(1)} %reshape.195) | copy-start | bytes 1572868
  83.6 19.8 %copy-start.25 = (bf16[16,16,8,128]{3,2,1,0:T(8,128)(2,1)S(1)}, bf16[16,16,8,128]{3,2,1,0:T(8,128)(2,1)}, u32[]{:S(2)}) copy-start(bf16[16,16,8,128]{3,2,1,0:T(8,128)(2,1)} %get-tuple-element.63) | copy-start | bytes 1572868
  103.4 2.0 copy-start.8
  103.4 2.0 copy-start.10
  103.4 3.4 %copy-start.13 = (bf16[16,128,1,128]{3,2,1,0:T(2,128)(2,1)}, bf16[16,128,1,128]{3,2,1,0:T(2,128)(2,1)S(1)}, u32[]{:S(2)}) copy-start(bf16[16,128,1,128]{3,2,1,0:T(2,128)(2,1)S(1)} %get-tuple-element.35) | copy-start | bytes 1572868
  103.4 4.6 %copy-start.12 = (bf16[16,128,1,128]{3,2,1,0:T(2,128)(2,1)}, bf16[16,128,1,128]{3,2,1,0:T(2,128)(2,1)S(1)}, u32[]{:S(2)}) copy-start(bf16[16,128,1,128]{3,2,1,0:T(2,128)(2,1)S(1)} %get-tuple-element.34) | copy-start | bytes 1572868
  103.4 5.1 %copy-start.4 = (bf16[16,128,1,128]{3,2,1,0:T(2,128)(2,1)}, bf16[16,128,1,128]{3,2,1,0:T(2,128)(2,1)S(1)}, u32[]{:S(2)}) copy-start(bf16[16,128,1,128]{3,2,1,0:T(2,128)(2,1)S(1)} %get-tuple-element.33) | copy-start | bytes 1572868
  103.4 6.1 %copy-start.2 = (bf16[16,128,1,128]{3,2,1,0:T(2,128)(2,1)}, bf16[16,128,1,128]{3,2,1,0:T(2,128)(2,1)S(1)}, u32[]{:S(2)}) copy-start(bf16[16,128,1,128]{3,2,1,0:T(2,128)(2,1)S(1)} %get-tuple-element.32) | copy-start | bytes 1572868
  103.4 7.6 %copy-start.16 = (bf16[16,128,1,128]{3,2,1,0:T(2,128)(2,1)}, bf16[16,128,1,128]{3,2,1,0:T(2,128)(2,1)S(1)}, u32[]{:S(2)}) copy-start(bf16[16,128,1,128]{3,2,1,0:T(2,128)(2,1)S(1)} %get-tuple-element.30) | copy-start | bytes 1572868
  113.1 14.5 %collective-permute-start.2 = (bf16[4,2048]{0,1:T(8,128)(2,1)S(1)}, bf16[4,2048]{0,1:T(8,128)(2,1)}, u32[]{:S(2)}, u32[]{:S(2)}) collective-permute-start(bf16[4,2048]{0,1:T(8,128)(2,1)S(1)} %copy.243), channel_id=1, source_target_pairs={{1,0},{2,1},{3,2},{4,3},{5,4},{6,5},{7,6},{9,8},{10,9},{11,10},{12... | collective-permute-start | bytes 49160 | tf_op jit(solution)/shard_map/ppermute | solution.py:20
  115.5 12.2 %collective-permute-start.3 = (bf16[4,2048]{0,1:T(8,128)(2,1)}, bf16[4,2048]{0,1:T(8,128)(2,1)}, u32[]{:S(2)}, u32[]{:S(2)}) collective-permute-start(bf16[4,2048]{0,1:T(8,128)(2,1)} %copy.253), channel_id=1, source_target_pairs={{0,1},{1,2},{2,3},{3,4},{4,5},{5,6},{6,7},{8,9},{9,10},{10,11},{11... | collective-permute-start | bytes 49160 | tf_op jit(solution)/shard_map/ppermute | solution.py:18
  123.1 23.8 %all-to-all-start.3 = ((bf16[128,8,256]{0,2,1:T(8,128)(2,1)}), bf16[128,8,256]{0,2,1:T(8,128)(2,1)}, u32[]{:S(2)}, u32[]{:S(2)}) async-start(bf16[128,8,256]{0,2,1:T(8,128)(2,1)} %bitcast.33), calls=%async_computation.3 | async-start | bytes 1048576 | tf_op jit(solution)/shard_map/all_to_all | solution.py:119
  127.7 6.5 %copy-start.11 = (bf16[16,128,1,128]{3,2,1,0:T(2,128)(2,1)S(1)}, bf16[16,128,1,128]{3,2,1,0:T(2,128)(2,1)}, u32[]{:S(2)}) copy-start(bf16[16,128,1,128]{3,2,1,0:T(2,128)(2,1)} %copy-done.10) | copy-start | bytes 1572868
  146.8 32.2 %all-to-all-start.1 = ((f32[4,65,2048]{2,1,0:T(8,128)}), f32[4,65,2048]{2,1,0:T(8,128)S(1)}, u32[]{:S(2)}, u32[]{:S(2)}) async-start(f32[4,65,2048]{2,1,0:T(8,128)} %select_maximum_fusion), calls=%async_computation.1 | async-start | bytes 4718592 | tf_op jit(solution)/shard_map/all_to_all | solution.py:57
  179.1 19.5 %all-to-all-start.5 = ((f32[4,64,1152]{2,1,0:T(8,128)}), f32[4,64,1152]{2,1,0:T(8,128)}, u32[]{:S(2)}, u32[]{:S(2)}) async-start(f32[4,64,1152]{2,1,0:T(8,128)} %mul.133), calls=%async_computation.5 | async-start | bytes 2359296 | tf_op jit(solution)/shard_map/all_to_all | solution.py:41
  198.6 30.9 %all-to-all-start.2 = ((f32[8,9,2048]{2,1,0:T(8,128)}), f32[8,9,2048]{2,1,0:T(8,128)S(1)}, u32[]{:S(2)}, u32[]{:S(2)}) async-start(f32[8,9,2048]{2,1,0:T(8,128)} %select_maximum_fusion.1), calls=%async_computation.2 | async-start | bytes 2097152 | tf_op jit(solution)/shard_map/all_to_all | solution.py:66
  230.6 18.6 %all-to-all-start.6 = ((f32[4,64,1152]{2,1,0:T(8,128)}), f32[4,64,1152]{2,1,0:T(8,128)S(1)}, u32[]{:S(2)}, u32[]{:S(2)}) async-start(f32[4,64,1152]{2,1,0:T(8,128)} %tile.5), calls=%async_computation.6 | async-start | bytes 2359296 | tf_op jit(solution)/shard_map/all_to_all | solution.py:35
  (21 other events, 25.6 us)
Sparse Core Ops, SparseCore 0:
  9.8 63.2 all-gather.1
where the time goes:
time: 259 us; the launch traced here: 257 us
  waiting for transfers between devices  96.4 us (37%)
  local copies, waits for them, and re-layouts  58.1 us (22%)
  starting transfers between devices  34.4 us (13%)
  blocking collectives  23.8 us (9%)
  matrix products  15.2 us (6%)
  between operations  14.7 us (6%)
  other arithmetic  14.6 us (6%)
    all_to_all x1, waiting for transfers between devices, scatter_terms(): second = lax.all_to_all(second, 'seq', 0, 0, tiled=True).sum(axis=0)  25.2 us
    all_to_all x1, blocking collectives, gather_rows(): return lax.all_to_all(jnp.tile(block, (count, 1)), axis, 0, 0, tiled=True)  23.8 us
    slice x1, local copies, waits for them, and re-layouts, body(): weights[:, :, k, :]  19.7 us
    all_to_all x1, waiting for transfers between devices, scatter_terms(): first = lax.all_to_all(first, 'fsdp', 0, 0, tiled=True).sum(axis=0)  17.9 us
    all_gather x1, waiting for transfers between devices, body(): lax.all_gather(kernel, 'fsdp', axis=0, tiled=True)  17.2 us
    unnamed x70, local copies, waits for them, and re-layouts  13.9 us
    all_to_all x1, waiting for transfers between devices, gather_rows(): return lax.all_to_all(jnp.tile(block, (count, 1)), axis, 0, 0, tiled=True)  13.9 us
    all_to_all x1, waiting for transfers between devices, sum_rows(): return lax.all_to_all(parts, axis, 0, 0, tiled=True).sum(axis=0)  13.9 us
  transfers between devices with their start and end apart: 11, of which 7 were waited for; matrix products, arithmetic and copies ran while one was open for 15% of the time, Pallas kernels for 0%

commit v1 on v0

--- a/solution.py
+++ b/solution.py
@@ -115,7 +115,10 @@
         )
     slice_width = width // seq_count
     normed_slice, dconv_slice = (
-        lax.all_to_all(normed, "seq", split_axis=1, concat_axis=0, tiled=True),
+        jnp.concatenate(
+            lax.all_to_all(jnp.stack(jnp.split(normed, lax.axis_size("seq"), axis=1)), "seq", 0, 0),
+            axis=0,
+        ),
         lax.all_to_all(dflat, "seq", split_axis=1, concat_axis=0, tiled=True),
     )
     whole = normed_slice.shape[0]

time: 259 us -> 260 us (level)
  local copies, waits for them, and re-layouts: 58.1 us -> 65.9 us
  waiting for transfers between devices: 96.4 us -> 90.5 us
    unnamed x70 -> x79, local copies, waits for them, and re-layouts: 13.9 us -> 18.7 us
    all_gather x1, waiting for transfers between devices: 17.2 us -> 13.6 us  [body(): lax.all_gather(kernel, 'fsdp', axis=0, tiled=True)]
    all_to_all x1, waiting for transfers between devices: 13.9 us -> 11.2 us  [sum_rows(): return lax.all_to_all(parts, axis, 0, 0, tiled=True).sum(axis=0)]
  transfers between devices with their start and end apart: 11 -> 11, of which waited for: 7 -> 7; matrix products, arithmetic and copies ran while one was open for 15% -> 18% of each run, Pallas kernels for 0% -> 0%
where the time goes in v1:
time: 260 us; the launch traced here: 258 us
  waiting for transfers between devices  90.5 us (35%)
  local copies, waits for them, and re-layouts  65.9 us (25%)
  starting transfers between devices  33.7 us (13%)
  blocking collectives  23.8 us (9%)
  matrix products  15.4 us (6%)
  between operations  14.7 us (6%)
  other arithmetic  14.4 us (6%)
    all_to_all x1, waiting for transfers between devices, scatter_terms(): second = lax.all_to_all(second, 'seq', 0, 0, tiled=True).sum(axis=0)  26.5 us
    all_to_all x1, blocking collectives, gather_rows(): return lax.all_to_all(jnp.tile(block, (count, 1)), axis, 0, 0, tiled=True)  23.8 us
    slice x1, local copies, waits for them, and re-layouts, body(): weights[:, :, k, :]  19.1 us
    unnamed x79, local copies, waits for them, and re-layouts  18.7 us
    all_to_all x1, waiting for transfers between devices, scatter_terms(): first = lax.all_to_all(first, 'fsdp', 0, 0, tiled=True).sum(axis=0)  17.1 us
    all_to_all x1, waiting for transfers between devices, gather_rows(): return lax.all_to_all(jnp.tile(block, (count, 1)), axis, 0, 0, tiled=True)  13.9 us
    all_gather x1, waiting for transfers between devices, body(): lax.all_gather(kernel, 'fsdp', axis=0, tiled=True)  13.6 us
    all_to_all x1, waiting for transfers between devices, sum_rows(): return lax.all_to_all(parts, axis, 0, 0, tiled=True).sum(axis=0)  11.2 us
  transfers between devices with their start and end apart: 11, of which 7 were waited for; matrix products, arithmetic and copies ran while one was open for 18% of the time, Pallas kernels for 0%

profile of v1, /device:TPU:0, one launch (start us, length us, event | category | flops | bytes accessed | tf_op | source)
XLA Modules:
  0.0 258.2 jit_solution(15934253683774970044)
XLA Ops:
  8.3 23.8 %all_to_all.54 = bf16[4,64,2048]{2,1,0:T(8,128)(2,1)S(1)} all-to-all(bf16[4,64,2048]{2,1,0:T(8,128)(2,1)S(1)} %tile.4), channel_id=1, replica_groups=mesh['fsdp'=4,'seq'=8] {'fsdp'}, dimensions={0} | all-to-all | bytes 2097152 | tf_op jit(solution)/shard_map/all_to_all | solution.py:35
  38.0 5.2 %all-to-all-start.4 = ((bf16[8,128,256]{2,1,0:T(8,128)(2,1)}), bf16[8,128,256]{2,1,0:T(8,128)(2,1)S(1)}, u32[]{:S(2)}, u32[]{:S(2)}) async-start(bf16[8,128,256]{2,1,0:T(8,128)(2,1)} %fusion.72), calls=%async_computation.4 | async-start | bytes 1048576 | tf_op jit(solution)/shard_map/all_to_all | solution.py:119
  43.1 2.4 collective-permute-start
  49.8 2.8 %fusion.52 = (bf16[16,16,8,128]{3,2,1,0:T(8,128)(2,1)}, bf16[16,16,8,128]{3,2,1,0:T(8,128)(2,1)}, bf16[16,16,8,128]{3,2,1,0:T(8,128)(2,1)}, bf16[16,16,8,128]{3,...) fusion(bf16[4,2048]{1,0:T(4,128)(2,1)S(1)} %collective-permute-, ...), kind=kLoop, calls=%fused_computation.112 | loop fusion | flops 8388608 | bytes 4751360
  52.5 5.9 %all-to-all-done.4 = bf16[8,128,256]{2,1,0:T(8,128)(2,1)S(1)} async-done(((bf16[8,128,256]{2,1,0:T(8,128)(2,1)}), bf16[8,128,256]{2,1,0:T(8,128)(2,1)S(1)}, u32[]{:S(2)}, u32[]{:S(2)}) %all-to-all-start.4) | async-done | bytes 524320 | tf_op jit(solution)/shard_map/all_to_all | solution.py:119
  59.6 13.6 %all-gather.2.cloned.1.call-done = bf16[2048,1152]{1,0:T(8,128)(2,1)} async-done(((bf16[512,1152]{1,0:T(8,128)(2,1)}), bf16[2048,1152]{1,0:T(8,128)(2,1)}) %all-gather.2.cloned.1.call-update) | async-done | bytes 4718608 | tf_op jit(solution)/shard_map/all_gather | solution.py:89
  73.1 10.5 %reshape.191 = bf16[16,128,9,128]{3,2,1,0:T(8,128)(2,1)} reshape(bf16[2048,1152]{1,0:T(8,128)(2,1)} %all-gather.2.cloned.1.call-done) | data formatting | bytes 9437184 | tf_op jit(solution)/shard_map/reshape | solution.py:89
  83.6 19.1 %fusion.91 = (bf16[16,128,1,128]{3,2,1,0:T(2,128)(2,1)S(1)}, bf16[16,128,1,128]{3,2,1,0:T(2,128)(2,1)S(1)}, bf16[16,128,1,128]{3,2,1,0:T(2,128)(2,1)S(1)}, bf16[...) fusion(bf16[16,128,9,128]{3,2,1,0:T(8,128)(2,1)} %reshape.191), kind=kLoop, calls=%fused_computation.177 | loop fusion | bytes 9437184 | tf_op jit(solution)/shard_map/slice | solution.py:97
  116.8 3.9 %collective-permute-start.3 = (bf16[4,2048]{0,1:T(8,128)(2,1)}, bf16[4,2048]{0,1:T(8,128)(2,1)}, u32[]{:S(2)}, u32[]{:S(2)}) collective-permute-start(bf16[4,2048]{0,1:T(8,128)(2,1)} %copy.202), channel_id=1, source_target_pairs={{0,1},{1,2},{2,3},{3,4},{4,5},{5,6},{6,7},{8,9},{9,10},{10,11},{11... | collective-permute-start | bytes 49160 | tf_op jit(solution)/shard_map/ppermute | solution.py:18
  120.7 2.9 %fusion.63 = f32[16,128,128]{1,2,0:T(8,128)} fusion(bf16[128,16,128]{2,0,1:T(8,128)(2,1)} %copy-done.14, bf16[16,128,1,128]{3,2,1,0:T(2,128)(2,1)} %copy-done.8), kind=kOutput, calls=%fused_computation.133 | convolution fusion | flops 67108864 | bytes 2097152 | tf_op jit(solution)/shard_map/tgo,goc->tgc/dot_general | solution.py:110
  123.6 2.0 copy.191
  125.6 4.6 %all-to-all-start.3 = ((bf16[128,8,256]{0,2,1:T(8,128)(2,1)}), bf16[128,8,256]{0,2,1:T(8,128)(2,1)}, u32[]{:S(2)}, u32[]{:S(2)}) async-start(bf16[128,8,256]{0,2,1:T(8,128)(2,1)} %bitcast.33), calls=%async_computation.3 | async-start | bytes 1048576 | tf_op jit(solution)/shard_map/all_to_all | solution.py:122
  130.3 6.7 %pad_maximum_fusion = (bf16[128,2048]{0,1:T(8,128)(2,1)S(1)}, bf16[128,2048]{0,1:T(8,128)(2,1)S(1)}, bf16[128,2048]{0,1:T(8,128)(2,1)S(1)}, bf16[128,2048]{0,1:T...) fusion(bf16[128,2048]{0,1:T(8,128)(2,1)} %bitcast.14, ...), kind=kLoop, calls=%fused_computation.109 | loop fusion | flops 8388608 | bytes 4751360 | tf_op jit(solution)/shard_map/concatenate | solution.py:16
  147.1 1.7 select_maximum_fusion
  148.8 3.6 %all-to-all-start.1 = ((f32[4,65,2048]{2,1,0:T(8,128)}), f32[4,65,2048]{2,1,0:T(8,128)S(1)}, u32[]{:S(2)}, u32[]{:S(2)}) async-start(f32[4,65,2048]{2,1,0:T(8,128)} %select_maximum_fusion), calls=%async_computation.1 | async-start | bytes 4718592 | tf_op jit(solution)/shard_map/all_to_all | solution.py:57
  159.3 2.1 copy.217
  161.4 2.5 mul.133
  163.9 17.1 %all-to-all-done.1 = f32[4,65,2048]{2,1,0:T(8,128)S(1)} async-done(((f32[4,65,2048]{2,1,0:T(8,128)}), f32[4,65,2048]{2,1,0:T(8,128)S(1)}, u32[]{:S(2)}, u32[]{:S(2)}) %all-to-all-start.1) | async-done | bytes 2129952 | tf_op jit(solution)/shard_map/all_to_all | solution.py:57
  181.0 3.5 %all-to-all-start.5 = ((f32[4,64,1152]{2,1,0:T(8,128)}), f32[4,64,1152]{2,1,0:T(8,128)S(1)}, u32[]{:S(2)}, u32[]{:S(2)}) async-start(f32[4,64,1152]{2,1,0:T(8,128)} %mul.133), calls=%async_computation.5 | async-start | bytes 2359296 | tf_op jit(solution)/shard_map/all_to_all | solution.py:41
  188.5 11.2 %all-to-all-done.5 = f32[4,64,1152]{2,1,0:T(8,128)S(1)} async-done(((f32[4,64,1152]{2,1,0:T(8,128)}), f32[4,64,1152]{2,1,0:T(8,128)S(1)}, u32[]{:S(2)}, u32[]{:S(2)}) %all-to-all-start.5) | async-done | bytes 1179680 | tf_op jit(solution)/shard_map/all_to_all | solution.py:41
  199.7 4.3 %all-to-all-start.2 = ((f32[8,9,2048]{2,1,0:T(8,128)}), f32[8,9,2048]{2,1,0:T(8,128)S(1)}, u32[]{:S(2)}, u32[]{:S(2)}) async-start(f32[8,9,2048]{2,1,0:T(8,128)} %select_maximum_fusion.1), calls=%async_computation.2 | async-start | bytes 2097152 | tf_op jit(solution)/shard_map/all_to_all | solution.py:66
  204.1 26.5 %all-to-all-done.2 = f32[8,9,2048]{2,1,0:T(8,128)S(1)} async-done(((f32[8,9,2048]{2,1,0:T(8,128)}), f32[8,9,2048]{2,1,0:T(8,128)S(1)}, u32[]{:S(2)}, u32[]{:S(2)}) %all-to-all-start.2) | async-done | bytes 589856 | tf_op jit(solution)/shard_map/all_to_all | solution.py:66
  231.7 3.5 %all-to-all-start.6 = ((f32[4,64,1152]{2,1,0:T(8,128)}), f32[4,64,1152]{2,1,0:T(8,128)S(1)}, u32[]{:S(2)}, u32[]{:S(2)}) async-start(f32[4,64,1152]{2,1,0:T(8,128)} %tile.5), calls=%async_computation.6 | async-start | bytes 2359296 | tf_op jit(solution)/shard_map/all_to_all | solution.py:35
  236.5 13.9 %all-to-all-done.6 = f32[4,64,1152]{2,1,0:T(8,128)S(1)} async-done(((f32[4,64,1152]{2,1,0:T(8,128)}), f32[4,64,1152]{2,1,0:T(8,128)S(1)}, u32[]{:S(2)}, u32[]{:S(2)}) %all-to-all-start.6) | async-done | bytes 1179680 | tf_op jit(solution)/shard_map/all_to_all | solution.py:35
  (145 shorter events, 50.3 us)
Async XLA Ops:
  7.2 66.0 %all-gather.2.cloned.1.call-start = ((), (), s32[]{:S(2)}) async-start(), calls=%async_computation.7 | async-start | bytes 5898240 | tf_op jit(solution)/shard_map/all_gather | solution.py:89
  8.2 23.8 %copy-start.28 = (bf16[1,128,2048]{2,1,0:T(8,128)(2,1)S(1)}, bf16[1,128,2048]{2,1,0:T(8,128)(2,1)}, u32[]{:S(2)}) copy-start(bf16[1,128,2048]{2,1,0:T(8,128)(2,1)} %param.10) | copy-start | bytes 1572868
  8.2 23.8 %copy-start.34 = (s32[1,128]{1,0:T(1,128)S(1)}, s32[1,128]{1,0:T(1,128)}, u32[]{:S(2)}) copy-start(s32[1,128]{1,0:T(1,128)} %param.11) | copy-start | bytes 1540
  32.9 14.0 %copy-start.15 = (bf16[1,128,2048]{2,1,0:T(8,128)(2,1)S(1)}, bf16[1,128,2048]{2,1,0:T(8,128)(2,1)}, u32[]{:S(2)}) copy-start(bf16[1,128,2048]{2,1,0:T(8,128)(2,1)} %param.15) | copy-start | bytes 1572868
  38.0 20.5 %all-to-all-start.4 = ((bf16[8,128,256]{2,1,0:T(8,128)(2,1)}), bf16[8,128,256]{2,1,0:T(8,128)(2,1)S(1)}, u32[]{:S(2)}, u32[]{:S(2)}) async-start(bf16[8,128,256]{2,1,0:T(8,128)(2,1)} %fusion.72), calls=%async_computation.4 | async-start | bytes 1048576 | tf_op jit(solution)/shard_map/all_to_all | solution.py:119
  43.1 5.0 %collective-permute-start = (bf16[4,2048]{1,0:T(4,128)(2,1)S(1)}, bf16[4,2048]{1,0:T(4,128)(2,1)S(1)}, u32[]{:S(2)}, u32[]{:S(2)}) collective-permute-start(bf16[4,2048]{1,0:T(4,128)(2,1)S(1)} %get-tuple-element.66), channel_id=1, source_target_pairs={{0,1},{1,2},{2,3},{3,4},{4,5},{5,6},{6,7},{8,9},{9,10},{10,11},{11... | collective-permute-start | bytes 49160 | tf_op jit(solution)/shard_map/ppermute | solution.py:18
  45.6 4.2 %collective-permute-start.1 = (bf16[4,2048]{1,0:T(4,128)(2,1)S(1)}, bf16[4,2048]{1,0:T(4,128)(2,1)S(1)}, u32[]{:S(2)}, u32[]{:S(2)}) collective-permute-start(bf16[4,2048]{1,0:T(4,128)(2,1)S(1)} %get-tuple-element.65), channel_id=1, source_target_pairs={{1,0},{2,1},{3,2},{4,3},{5,4},{6,5},{7,6},{9,8},{10,9},{11,10},{12... | collective-permute-start | bytes 49160 | tf_op jit(solution)/shard_map/ppermute | solution.py:20
  58.6 14.5 %copy-start.17 = (bf16[1024,2,128]{2,1,0:T(2,128)(2,1)}, bf16[1024,2,128]{2,1,0:T(2,128)(2,1)S(1)}, u32[]{:S(2)}) copy-start(bf16[1024,2,128]{2,1,0:T(2,128)(2,1)S(1)} %reshape_reshape.3) | copy-start | bytes 1572868
  83.6 19.2 %copy-start.25 = (bf16[16,16,8,128]{3,2,1,0:T(8,128)(2,1)S(1)}, bf16[16,16,8,128]{3,2,1,0:T(8,128)(2,1)}, u32[]{:S(2)}) copy-start(bf16[16,16,8,128]{3,2,1,0:T(8,128)(2,1)} %get-tuple-element.63) | copy-start | bytes 1572868
  102.8 2.0 copy-start.4
  102.8 2.0 copy-start.6
  102.8 3.4 %copy-start.9 = (bf16[16,128,1,128]{3,2,1,0:T(2,128)(2,1)}, bf16[16,128,1,128]{3,2,1,0:T(2,128)(2,1)S(1)}, u32[]{:S(2)}) copy-start(bf16[16,128,1,128]{3,2,1,0:T(2,128)(2,1)S(1)} %get-tuple-element.35) | copy-start | bytes 1572868
  102.8 4.4 %copy-start.8 = (bf16[16,128,1,128]{3,2,1,0:T(2,128)(2,1)}, bf16[16,128,1,128]{3,2,1,0:T(2,128)(2,1)S(1)}, u32[]{:S(2)}) copy-start(bf16[16,128,1,128]{3,2,1,0:T(2,128)(2,1)S(1)} %get-tuple-element.34) | copy-start | bytes 1572868
  102.8 5.0 %copy-start = (bf16[16,128,1,128]{3,2,1,0:T(2,128)(2,1)}, bf16[16,128,1,128]{3,2,1,0:T(2,128)(2,1)S(1)}, u32[]{:S(2)}) copy-start(bf16[16,128,1,128]{3,2,1,0:T(2,128)(2,1)S(1)} %get-tuple-element.33) | copy-start | bytes 1572868
  102.8 8.0 %copy-start.12 = (bf16[16,128,1,128]{3,2,1,0:T(2,128)(2,1)}, bf16[16,128,1,128]{3,2,1,0:T(2,128)(2,1)S(1)}, u32[]{:S(2)}) copy-start(bf16[16,128,1,128]{3,2,1,0:T(2,128)(2,1)S(1)} %get-tuple-element.30) | copy-start | bytes 1572868
  114.5 15.7 %collective-permute-start.2 = (bf16[4,2048]{0,1:T(8,128)(2,1)}, bf16[4,2048]{0,1:T(8,128)(2,1)}, u32[]{:S(2)}, u32[]{:S(2)}) collective-permute-start(bf16[4,2048]{0,1:T(8,128)(2,1)} %copy.192), channel_id=1, source_target_pairs={{1,0},{2,1},{3,2},{4,3},{5,4},{6,5},{7,6},{9,8},{10,9},{11,10},{12... | collective-permute-start | bytes 49160 | tf_op jit(solution)/shard_map/ppermute | solution.py:20
  116.8 13.4 %collective-permute-start.3 = (bf16[4,2048]{0,1:T(8,128)(2,1)}, bf16[4,2048]{0,1:T(8,128)(2,1)}, u32[]{:S(2)}, u32[]{:S(2)}) collective-permute-start(bf16[4,2048]{0,1:T(8,128)(2,1)} %copy.202), channel_id=1, source_target_pairs={{0,1},{1,2},{2,3},{3,4},{4,5},{5,6},{6,7},{8,9},{9,10},{10,11},{11... | collective-permute-start | bytes 49160 | tf_op jit(solution)/shard_map/ppermute | solution.py:18
  125.6 23.2 %all-to-all-start.3 = ((bf16[128,8,256]{0,2,1:T(8,128)(2,1)}), bf16[128,8,256]{0,2,1:T(8,128)(2,1)}, u32[]{:S(2)}, u32[]{:S(2)}) async-start(bf16[128,8,256]{0,2,1:T(8,128)(2,1)} %bitcast.33), calls=%async_computation.3 | async-start | bytes 1048576 | tf_op jit(solution)/shard_map/all_to_all | solution.py:122
  130.2 6.7 %copy-start.7 = (bf16[16,128,1,128]{3,2,1,0:T(2,128)(2,1)S(1)}, bf16[16,128,1,128]{3,2,1,0:T(2,128)(2,1)}, u32[]{:S(2)}) copy-start(bf16[16,128,1,128]{3,2,1,0:T(2,128)(2,1)} %copy-done.6) | copy-start | bytes 1572868
  148.8 32.2 %all-to-all-start.1 = ((f32[4,65,2048]{2,1,0:T(8,128)}), f32[4,65,2048]{2,1,0:T(8,128)S(1)}, u32[]{:S(2)}, u32[]{:S(2)}) async-start(f32[4,65,2048]{2,1,0:T(8,128)} %select_maximum_fusion), calls=%async_computation.1 | async-start | bytes 4718592 | tf_op jit(solution)/shard_map/all_to_all | solution.py:57
  152.4 2.5 copy-start.30
  181.0 18.7 %all-to-all-start.5 = ((f32[4,64,1152]{2,1,0:T(8,128)}), f32[4,64,1152]{2,1,0:T(8,128)S(1)}, u32[]{:S(2)}, u32[]{:S(2)}) async-start(f32[4,64,1152]{2,1,0:T(8,128)} %mul.133), calls=%async_computation.5 | async-start | bytes 2359296 | tf_op jit(solution)/shard_map/all_to_all | solution.py:41
  199.7 30.9 %all-to-all-start.2 = ((f32[8,9,2048]{2,1,0:T(8,128)}), f32[8,9,2048]{2,1,0:T(8,128)S(1)}, u32[]{:S(2)}, u32[]{:S(2)}) async-start(f32[8,9,2048]{2,1,0:T(8,128)} %select_maximum_fusion.1), calls=%async_computation.2 | async-start | bytes 2097152 | tf_op jit(solution)/shard_map/all_to_all | solution.py:66
  231.7 18.6 %all-to-all-start.6 = ((f32[4,64,1152]{2,1,0:T(8,128)}), f32[4,64,1152]{2,1,0:T(8,128)S(1)}, u32[]{:S(2)}, u32[]{:S(2)}) async-start(f32[4,64,1152]{2,1,0:T(8,128)} %tile.5), calls=%async_computation.6 | async-start | bytes 2359296 | tf_op jit(solution)/shard_map/all_to_all | solution.py:35
  (22 other events, 26.0 us)
Sparse Core Ops, SparseCore 0:
  9.8 63.2 all-gather.1
